TPU v7x, 32 devices: a whole 2x2x4 slice. The times are simulated.
32 devices in a mesh: dp: 8 (over z, y), tensor: 4 (over x, core).
Axes of the slice: x: 2, y: 2, z: 4, core: 2. Of those that a mesh axis runs over, the one named last changes fastest.
Arguments:
- inputs: bfloat16 [1024, 8192], P('dp', 'tensor'), may hold values from -6 to 6
- cotangent: bfloat16 [1024, 1024], P('dp', 'tensor'), may hold values from -6 to 6
- frozen_key_weight: bfloat16 [8192, 1024], P(None, 'tensor'), may hold values from -0.1875 to 0.1875
- adapter_down_weight: bfloat16 [8, 16, 8192], P('dp', None, 'tensor'), may hold values from -0.0625 to 0.0625
- adapter_up_weight: bfloat16 [8, 16, 1024], P('dp', None, 'tensor'), may hold values from -0.1875 to 0.1875
- tenant_per_block: int32 [8], P('dp'), may hold values from 0 to 7
Outputs:
- grad_inputs: bfloat16 [1024, 8192], P('dp', 'tensor')
- grad_down: float32 [8, 16, 8192], P('dp', None, 'tensor')
- grad_up: float32 [8, 16, 1024], P('dp', None, 'tensor')
All inputs are finite; a program needn't handle non-finite values.
Results may differ from a plain program's by a relative error of at most 0.0034.
Values may be sent and summed in bfloat16 or wider, within the bound.
No kernel may reach another device: no remote copies, remote signals or barrier semaphores. Data moves between devices by JAX's collectives and lax.ppermute only.
A program may use at most 128 MiB of HBM per device.

v0:
```python
import jax
import jax.numpy as jnp
from jax import lax
from jax.sharding import PartitionSpec as P

ADAPTER_SCALE = 2.0


def on_device(
    inputs, cotangent, frozen_key_weight, adapter_down_weight, adapter_up_weight, tenant_per_block
):
    token_row_count, width_portion = inputs.shape
    key_portion = cotangent.shape[1]
    block_count = tenant_per_block.shape[0]
    block_rows = token_row_count // block_count
    adapter_rank_size = adapter_down_weight.shape[1]
    held_block_count = adapter_down_weight.shape[0]
    owner_count = lax.axis_size("dp")
    tenant_number = owner_count * held_block_count
    pieces = (
        lax.all_gather(adapter_down_weight, "dp", axis=0, tiled=True),
        lax.all_gather(adapter_up_weight, "dp", axis=0, tiled=True),
    )
    piece_count = pieces[0].shape[0]
    tenant_ids = jnp.arange(piece_count, dtype=jnp.int32)
    member = (tenant_per_block[:, None] == tenant_ids[None, :]).astype(jnp.bfloat16)
    down_sum = jnp.einsum("bk,krd->brd", member, pieces[0], preferred_element_type=jnp.float32)
    up_sum = jnp.einsum("bk,krd->brd", member, pieces[1], preferred_element_type=jnp.float32)
    sel_down = down_sum
    sel_up = up_sum
    sel_down = sel_down.astype(jnp.bfloat16)
    sel_up = sel_up.astype(jnp.bfloat16)
    input_blocks = inputs.reshape(block_count, block_rows, width_portion)
    cotangent_blocks = cotangent.reshape(block_count, block_rows, key_portion)
    low_in = jnp.einsum("bnd,brd->bnr", input_blocks, sel_down, preferred_element_type=jnp.float32)
    reduced_output = ADAPTER_SCALE * jnp.einsum(
        "bnk,brk->bnr", cotangent_blocks, sel_up, preferred_element_type=jnp.float32
    )
    low_in, reduced_output = lax.psum((low_in, reduced_output), "tensor")
    reduced_input_batch = low_in.astype(jnp.bfloat16)
    low_out_b = reduced_output.astype(jnp.bfloat16)
    adapter_grad = jnp.einsum(
        "bnr,brd->bnd", low_out_b, sel_down, preferred_element_type=jnp.float32
    )
    adapter_grad = adapter_grad.reshape(token_row_count, width_portion)
    partial_grad = lax.dot_general(
        cotangent, frozen_key_weight, (((1,), (1,)), ((), ())), preferred_element_type=jnp.float32
    )
    base_grad = lax.psum_scatter(partial_grad, "tensor", scatter_dimension=1, tiled=True)
    grad_inputs = (base_grad + adapter_grad).astype(jnp.bfloat16)
    all_tenants = jnp.arange(tenant_number, dtype=jnp.int32)
    member = tenant_per_block[:, None] == all_tenants[None, :]
    member_b = member.astype(jnp.bfloat16)
    weighted_out = (member_b[:, None, :, None] * low_out_b[:, :, None, :]).reshape(
        token_row_count, tenant_number * adapter_rank_size
    )
    weighted_in = (member_b[:, None, :, None] * reduced_input_batch[:, :, None, :]).reshape(
        token_row_count, tenant_number * adapter_rank_size
    )
    down_contribution = lax.dot_general(
        weighted_out, inputs, (((0,), (0,)), ((), ())), preferred_element_type=jnp.float32
    )
    up_contribution = ADAPTER_SCALE * lax.dot_general(
        weighted_in, cotangent, (((0,), (0,)), ((), ())), preferred_element_type=jnp.float32
    )
    down_contribution = down_contribution.reshape(tenant_number, adapter_rank_size, width_portion)
    up_contribution = up_contribution.reshape(tenant_number, adapter_rank_size, key_portion)
    combined = jnp.concatenate([down_contribution, up_contribution], axis=2)
    owned = lax.psum_scatter(combined, "dp", scatter_dimension=0, tiled=True)
    grad_down = owned[:, :, :width_portion]
    grad_up = owned[:, :, width_portion:]
    return (grad_inputs, grad_down, grad_up)


def solution(mesh):
    in_specs = (
        P("dp", "tensor"),
        P("dp", "tensor"),
        P(None, "tensor"),
        P("dp", None, "tensor"),
        P("dp", None, "tensor"),
        P("dp"),
    )
    out_specs = (P("dp", "tensor"), P("dp", None, "tensor"), P("dp", None, "tensor"))
    return jax.shard_map(
        on_device, mesh=mesh, in_specs=in_specs, out_specs=out_specs, check_vma=False
    )
```

profile of v0, /device:TPU:0, one launch (start us, length us, event | category | flops | bytes accessed | tf_op | source)
XLA Modules:
  0.0 207.2 jit_solution(9838430073450406495)
XLA Ops:
  7.2 0.0 copy-start
  7.2 0.0 copy-start.1
  7.2 0.0 reduce-scatter.5.cloned.1.call-start
  7.2 33.3 %all_gather.7 = bf16[8,16,2048]{2,1,0:T(8,128)(2,1)S(1)} all-gather(bf16[1,16,2048]{2,1,0:T(8,128)(2,1)} %param.9), channel_id=1, replica_groups=mesh['dp'=8,'tensor'=4] {'dp'}, dimensions={0}, use_global_device_ids=true | all-gather | bytes 589824 | tf_op jit(solution)/shard_map/all_gather | solution.py:21
  41.2 30.7 %all_gather.6 = bf16[8,16,256]{2,1,0:T(8,128)(2,1)S(1)} all-gather(bf16[1,16,256]{2,1,0:T(8,128)(2,1)} %param.10), channel_id=1, replica_groups=mesh['dp'=8,'tensor'=4] {'dp'}, dimensions={0}, use_global_device_ids=true | all-gather | bytes 73728 | tf_op jit(solution)/shard_map/all_gather | solution.py:22
  72.0 0.1 mul.62
  72.0 0.1 mul.63
  72.1 0.5 fusion.4
  72.6 0.1 fusion.6
  72.7 1.0 fusion.1
  73.7 0.0 copy-done
  73.7 0.3 convolution_bitcast_fusion
  74.0 10.2 %all-reduce = (bf16[1,128,16]{1,2,0:T(8,128)(2,1)S(1)}, bf16[1,128,16]{1,2,0:T(8,128)(2,1)S(1)}) all-reduce(f32[1,128,16]{1,2,0:T(8,128)S(1)} %fusion.1, f32[1,128,16]{1,2,0:T(8,128)S(1)} %convolution_bitcast_fusion), channel_id=1, replica_groups=mesh['dp'=8,'tensor'=4] {'tensor'}, use_global_device_ids=true, to_apply=%region_1.0 | all-reduce | flops 4096 | bytes 24576 | tf_op jit(solution)/shard_map/psum | solution.py:39
  84.1 0.1 bitcast_multiply_fusion.1
  84.2 1.0 convolution_multiply_fusion
  85.2 0.3 fusion.2
  85.5 1.1 pad_maximum_fusion
  86.6 0.0 reduce-scatter.5.cloned.1.call-update
  86.6 0.0 reduce-scatter.3.cloned.1.call-start
  86.7 0.0 copy-done.1
  86.7 5.6 %fusion.14 = f32[128,8192]{1,0:T(8,128)} fusion(bf16[128,256]{1,0:T(8,128)(2,1)S(1)} %copy-done.1, bf16[8192,256]{1,0:T(8,128)(2,1)} %param.8), kind=kOutput, calls=%fused_computation.26 | convolution fusion | flops 536870912 | bytes 8454144 | tf_op jit(solution)/shard_map/dot_general | solution.py:46
  92.3 0.0 reduce-scatter.3.cloned.1.call-update
  92.3 59.7 %reduce-scatter.5.cloned.1.call-done = f32[1,16,2304]{2,1,0:T(8,128)} async-done(((f32[8,16,2304]{2,1,0:T(8,128)}), f32[1,16,2304]{2,1,0:T(8,128)}) %reduce-scatter.5.cloned.1.call-update) | async-done | bytes 147472 | tf_op jit(solution)/shard_map/reduce_scatter | solution.py:69
  152.0 1.6 slice.8
  153.6 1.3 slice.9
  154.9 43.1 %reduce-scatter.3.cloned.1.call-done = f32[128,2048]{1,0:T(8,128)} async-done(((f32[128,8192]{1,0:T(8,128)}), f32[128,2048]{1,0:T(8,128)}) %reduce-scatter.3.cloned.1.call-update) | async-done | bytes 1048592 | tf_op jit(solution)/shard_map/reduce_scatter | solution.py:49
  198.0 2.3 %fusion = bf16[128,2048]{1,0:T(8,128)(2,1)} fusion(f32[128,2048]{1,0:T(8,128)} %reduce-scatter.3.cloned.1.call-done, bf16[1,16,2048]{2,0,1:T(2,128)(2,1)S(1)} %fusion.4, bf16[1,128,16]{1,2,0:T(8,128)(2,1)S(1)} %get-tuple-element.3), kind=kOutput, calls=%fused_computation.1 | convolution fusion | flops 8912896 | bytes 1642496 | tf_op jit(solution)/shard_map/bnr,brd->bnd/dot_general | solution.py:42
  (1 shorter events, 0.0 us)
Async XLA Ops:
  7.2 66.5 %copy-start = (bf16[128,2048]{1,0:T(8,128)(2,1)S(1)}, bf16[128,2048]{1,0:T(8,128)(2,1)}, u32[]{:S(2)}) copy-start(bf16[128,2048]{1,0:T(8,128)(2,1)} %param.6) | copy-start | bytes 1572868
  7.2 79.5 %copy-start.1 = (bf16[128,256]{1,0:T(8,128)(2,1)S(1)}, bf16[128,256]{1,0:T(8,128)(2,1)}, u32[]{:S(2)}) copy-start(bf16[128,256]{1,0:T(8,128)(2,1)} %param.7) | copy-start | bytes 196612
  7.2 144.8 %reduce-scatter.5.cloned.1.call-start = ((), (), s32[]{:S(2)}) async-start(), calls=%async_computation.3 | async-start | bytes 1327104 | tf_op jit(solution)/shard_map/reduce_scatter | solution.py:69
  86.6 111.4 %reduce-scatter.3.cloned.1.call-start = ((), (), s32[]{:S(2)}) async-start(), calls=%async_computation.2 | async-start | bytes 5242880 | tf_op jit(solution)/shard_map/reduce_scatter | solution.py:49
Sparse Core Ops, SparseCore 0:
  86.7 65.2 reduce-scatter.4
  154.5 43.4 reduce-scatter.2
where the time goes:
time: 208 us; the launch traced here: 207 us
  waiting for transfers between devices  103 us (50%)
  blocking collectives  74.2 us (36%)
  between operations  14.7 us (7%)
  matrix products  11.1 us (5%)
  local copies, waits for them, and re-layouts  3.07 us (1%)
    reduce_scatter x1, waiting for transfers between devices, on_device(): owned = lax.psum_scatter(combined, 'dp', scatter_dimension=0, tiled=True)  59.7 us
    reduce_scatter x1, waiting for transfers between devices, on_device(): lax.psum_scatter(partial_grad, 'tensor', scatter_dimension=1, tiled=True)  43.1 us
    all_gather x1, blocking collectives, on_device(): lax.all_gather(adapter_down_weight, 'dp', axis=0, tiled=True)  33.3 us
    all_gather x1, blocking collectives, on_device(): lax.all_gather(adapter_up_weight, 'dp', axis=0, tiled=True)  30.7 us
    psum x1, blocking collectives, on_device(): low_in, reduced_output = lax.psum((low_in, reduced_output), 'tensor')  10.2 us
    dot_general x1, matrix products, on_device(): lax.dot_general(cotangent, frozen_key_weight, (((1,), (1,)), ((), ())), p...  5.61 us
  transfers between devices with their start and end apart: 2, of which 2 were waited for; matrix products, arithmetic and copies ran while one was open for 4% of the time, Pallas kernels for 0%

commit v1 on v0

--- a/solution.py
+++ b/solution.py
@@ -4,6 +4,18 @@
 from jax.sharding import PartitionSpec as P
 
 ADAPTER_SCALE = 2.0
+
+
+def doubled_up(x, axis, dim):
+    ways, here, step = (lax.axis_size(axis), lax.axis_index(axis), x.shape[dim])
+    line, have = (x, 1)
+    while have < ways:
+        line = jnp.concatenate(
+            [line, lax.ppermute(line, axis, [(d, (d - have) % ways) for d in range(ways)])],
+            axis=dim,
+        )
+        have = 2 * have
+    return jnp.roll(line, here * step, axis=dim)
 
 
 def on_device(
@@ -18,7 +30,7 @@
     owner_count = lax.axis_size("dp")
     tenant_number = owner_count * held_block_count
     pieces = (
-        lax.all_gather(adapter_down_weight, "dp", axis=0, tiled=True),
+        doubled_up(adapter_down_weight, "dp", 0),
         lax.all_gather(adapter_up_weight, "dp", axis=0, tiled=True),
     )
     piece_count = pieces[0].shape[0]

time: 208 us -> 195 us (0.938)
  blocking collectives: 74.2 us -> 40.9 us
  waiting for transfers between devices: 103 us -> 113 us
  starting transfers between devices: 0.08 us -> 8.12 us
    all_gather x1 -> x0, blocking collectives: 33.3 us -> none  [on_device(): lax.all_gather(adapter_down_weight, 'dp', axis=0, tiled=True)]
    ppermute x0 -> x3, waiting for transfers between devices: none -> 12.3 us  [doubled_up(): lax.ppermute(line, axis, [(d, (d - have) % ways) for d in range(ways)])]
    ppermute x0 -> x3, starting transfers between devices: none -> 8.04 us  [doubled_up(): lax.ppermute(line, axis, [(d, (d - have) % ways) for d in range(ways)])]
    reduce_scatter x1, waiting for transfers between devices: 59.7 us -> 57.5 us  [on_device(): owned = lax.psum_scatter(combined, 'dp', scatter_dimension=0, tiled=True)]
  transfers between devices with their start and end apart: 2 -> 5, of which waited for: 2 -> 4; matrix products, arithmetic and copies ran while one was open for 4% -> 5% of each run, Pallas kernels for 0% -> 0%
where the time goes in v1:
time: 195 us
  waiting for transfers between devices  113 us (58%)
  blocking collectives  40.9 us (21%)
  between operations  14.8 us (8%)
  matrix products  10.2 us (5%)
  starting transfers between devices  8.12 us (4%)
  local copies, waits for them, and re-layouts  4.88 us (3%)
  other arithmetic  2.9 us (1%)
    reduce_scatter x1, waiting for transfers between devices, on_device(): owned = lax.psum_scatter(combined, 'dp', scatter_dimension=0, tiled=True)  57.5 us
    reduce_scatter x1, waiting for transfers between devices, on_device(): lax.psum_scatter(partial_grad, 'tensor', scatter_dimension=1, tiled=True)  43.2 us
    all_gather x1, blocking collectives, on_device(): lax.all_gather(adapter_up_weight, 'dp', axis=0, tiled=True)  30.7 us
    ppermute x3, waiting for transfers between devices, doubled_up(): lax.ppermute(line, axis, [(d, (d - have) % ways) for d in range(ways)])  12.3 us
    psum x1, blocking collectives, on_device(): low_in, reduced_output = lax.psum((low_in, reduced_output), 'tensor')  10.2 us
    ppermute x3, starting transfers between devices, doubled_up(): lax.ppermute(line, axis, [(d, (d - have) % ways) for d in range(ways)])  8.04 us
    dot_general x1, matrix products, on_device(): lax.dot_general(cotangent, frozen_key_weight, (((1,), (1,)), ((), ())), p...  5.61 us
  transfers between devices with their start and end apart: 5, of which 4 were waited for; matrix products, arithmetic and copies ran while one was open for 5% of the time, Pallas kernels for 0%

profile of v1, /device:TPU:0, one launch (start us, length us, event | category | flops | bytes accessed | tf_op | source)
XLA Modules:
  0.0 194.9 jit_solution(2853137321437586871)
XLA Ops:
  7.2 0.0 copy-start
  7.2 0.0 reduce-scatter.5.cloned.1.call-start
  7.2 6.1 %collective-permute-start = (bf16[1,16,2048]{2,1,0:T(8,128)(2,1)}, bf16[1,16,2048]{2,1,0:T(8,128)(2,1)S(1)}, u32[]{:S(2)}, u32[]{:S(2)}) collective-permute-start(bf16[1,16,2048]{2,1,0:T(8,128)(2,1)} %param.9), channel_id=1, source_target_pairs={{0,28},{4,0},{8,4},{12,8},{16,12},{20,16},{24,20},{28,24},{1,29},{... | collective-permute-start | bytes 196616 | tf_op jit(solution)/shard_map/ppermute | solution.py:14
  13.9 30.7 %all_gather.3 = bf16[8,16,256]{2,1,0:T(8,128)(2,1)S(1)} all-gather(bf16[1,16,256]{2,1,0:T(8,128)(2,1)} %param.10), channel_id=1, replica_groups=mesh['dp'=8,'tensor'=4] {'dp'}, dimensions={0}, use_global_device_ids=true | all-gather | bytes 73728 | tf_op jit(solution)/shard_map/all_gather | solution.py:34
  44.7 0.1 fusion.6
  44.8 0.8 constant_dynamic-update-slice_fusion.7
  45.7 0.9 pad_maximum_fusion.2
  46.5 0.6 collective-permute-start.1
  47.1 0.1 mul.62
  47.2 0.1 mul.63
  47.3 1.0 fusion.1
  48.3 3.6 %collective-permute-done.1 = bf16[2,16,2048]{2,1,0:T(8,128)(2,1)S(1)} collective-permute-done((bf16[2,16,2048]{2,1,0:T(8,128)(2,1)S(1)}, bf16[2,16,2048]{2,1,0:T(8,128)(2,1)S(1)}, u32[]{:S(2)}, u32[]{:S(2)}) %collective-permute-start.1) | collective-permute-done | bytes 131104 | tf_op jit(solution)/shard_map/ppermute | solution.py:14
  51.9 0.9 pad_maximum_fusion.1
  52.7 1.4 collective-permute-start.2
  54.1 8.8 %collective-permute-done.2 = bf16[4,16,2048]{2,1,0:T(8,128)(2,1)S(1)} collective-permute-done((bf16[4,16,2048]{2,1,0:T(8,128)(2,1)S(1)}, bf16[4,16,2048]{2,1,0:T(8,128)(2,1)S(1)}, u32[]{:S(2)}, u32[]{:S(2)}) %collective-permute-start.2) | collective-permute-done | bytes 262176 | tf_op jit(solution)/shard_map/ppermute | solution.py:14
  62.9 0.8 constant_dynamic-update-slice_fusion.3
  63.9 0.4 fusion.4
  64.3 0.2 convolution_bitcast_fusion
  64.6 10.2 %all-reduce = (bf16[1,128,16]{1,2,0:T(8,128)(2,1)S(1)}, bf16[1,128,16]{1,2,0:T(8,128)(2,1)S(1)}) all-reduce(f32[1,128,16]{1,2,0:T(8,128)S(1)} %fusion.1, f32[1,128,16]{1,2,0:T(8,128)S(1)} %convolution_bitcast_fusion), channel_id=1, replica_groups=mesh['dp'=8,'tensor'=4] {'tensor'}, use_global_device_ids=true, to_apply=%region_1.2 | all-reduce | flops 4096 | bytes 24576 | tf_op jit(solution)/shard_map/psum | solution.py:51
  74.7 0.1 bitcast_multiply_fusion.1
  74.8 0.2 convolution_multiply_fusion
  75.0 0.3 fusion.2
  75.3 1.1 pad_maximum_fusion
  76.4 0.0 reduce-scatter.5.cloned.1.call-update
  76.4 0.0 reduce-scatter.3.cloned.1.call-start
  76.5 5.6 %fusion.14 = f32[128,8192]{1,0:T(8,128)} fusion(bf16[128,256]{1,0:T(8,128)(2,1)S(1)} %copy-done.1, bf16[8192,256]{1,0:T(8,128)(2,1)} %param.8), kind=kOutput, calls=%fused_computation.37 | convolution fusion | flops 536870912 | bytes 8454144 | tf_op jit(solution)/shard_map/dot_general | solution.py:58
  82.1 0.0 reduce-scatter.3.cloned.1.call-update
  82.1 57.5 %reduce-scatter.5.cloned.1.call-done = f32[1,16,2304]{2,1,0:T(8,128)} async-done(((f32[8,16,2304]{2,1,0:T(8,128)}), f32[1,16,2304]{2,1,0:T(8,128)}) %reduce-scatter.5.cloned.1.call-update) | async-done | bytes 147472 | tf_op jit(solution)/shard_map/reduce_scatter | solution.py:81
  139.6 1.6 slice.8
  141.2 1.3 slice.9
  142.5 43.2 %reduce-scatter.3.cloned.1.call-done = f32[128,2048]{1,0:T(8,128)} async-done(((f32[128,8192]{1,0:T(8,128)}), f32[128,2048]{1,0:T(8,128)}) %reduce-scatter.3.cloned.1.call-update) | async-done | bytes 1048592 | tf_op jit(solution)/shard_map/reduce_scatter | solution.py:61
  185.7 2.3 %fusion = bf16[128,2048]{1,0:T(8,128)(2,1)} fusion(f32[128,2048]{1,0:T(8,128)} %reduce-scatter.3.cloned.1.call-done, bf16[1,16,2048]{2,0,1:T(2,128)(2,1)S(1)} %fusion.4, bf16[1,128,16]{1,2,0:T(8,128)(2,1)S(1)} %get-tuple-element.3), kind=kOutput, calls=%fused_computation.1 | convolution fusion | flops 8912896 | bytes 1642496 | tf_op jit(solution)/shard_map/bnr,brd->bnd/dot_general | solution.py:54
  (12 shorter events, 0.1 us)
Async XLA Ops:
  7.2 57.1 %copy-start = (bf16[128,2048]{1,0:T(8,128)(2,1)S(1)}, bf16[128,2048]{1,0:T(8,128)(2,1)}, u32[]{:S(2)}) copy-start(bf16[128,2048]{1,0:T(8,128)(2,1)} %param.6) | copy-start | bytes 1572868
  7.2 67.6 %copy-start.1 = (bf16[128,256]{1,0:T(8,128)(2,1)S(1)}, bf16[128,256]{1,0:T(8,128)(2,1)}, u32[]{:S(2)}) copy-start(bf16[128,256]{1,0:T(8,128)(2,1)} %param.7) | copy-start | bytes 196612
  7.2 132.4 %reduce-scatter.5.cloned.1.call-start = ((), (), s32[]{:S(2)}) async-start(), calls=%async_computation.3 | async-start | bytes 1327104 | tf_op jit(solution)/shard_map/reduce_scatter | solution.py:81
  7.2 38.4 %collective-permute-start = (bf16[1,16,2048]{2,1,0:T(8,128)(2,1)}, bf16[1,16,2048]{2,1,0:T(8,128)(2,1)S(1)}, u32[]{:S(2)}, u32[]{:S(2)}) collective-permute-start(bf16[1,16,2048]{2,1,0:T(8,128)(2,1)} %param.9), channel_id=1, source_target_pairs={{0,28},{4,0},{8,4},{12,8},{16,12},{20,16},{24,20},{28,24},{1,29},{... | collective-permute-start | bytes 196616 | tf_op jit(solution)/shard_map/ppermute | solution.py:14
  46.5 5.3 %collective-permute-start.1 = (bf16[2,16,2048]{2,1,0:T(8,128)(2,1)S(1)}, bf16[2,16,2048]{2,1,0:T(8,128)(2,1)S(1)}, u32[]{:S(2)}, u32[]{:S(2)}) collective-permute-start(bf16[2,16,2048]{2,1,0:T(8,128)(2,1)S(1)} %pad_maximum_fusion.2), channel_id=1, source_target_pairs={{0,24},{4,28},{8,0},{12,4},{16,8},{20,12},{24,16},{28,20},{1,25},{... | collective-permute-start | bytes 393224 | tf_op jit(solution)/shard_map/ppermute | solution.py:14
  52.7 10.1 %collective-permute-start.2 = (bf16[4,16,2048]{2,1,0:T(8,128)(2,1)S(1)}, bf16[4,16,2048]{2,1,0:T(8,128)(2,1)S(1)}, u32[]{:S(2)}, u32[]{:S(2)}) collective-permute-start(bf16[4,16,2048]{2,1,0:T(8,128)(2,1)S(1)} %pad_maximum_fusion.1), channel_id=1, source_target_pairs={{0,16},{4,20},{8,24},{12,28},{16,0},{20,4},{24,8},{28,12},{1,17},{... | collective-permute-start | bytes 786440 | tf_op jit(solution)/shard_map/ppermute | solution.py:14
  76.4 109.3 %reduce-scatter.3.cloned.1.call-start = ((), (), s32[]{:S(2)}) async-start(), calls=%async_computation.2 | async-start | bytes 5242880 | tf_op jit(solution)/shard_map/reduce_scatter | solution.py:61
Sparse Core Ops, SparseCore 0:
  76.5 63.0 reduce-scatter.4
  142.1 43.5 reduce-scatter.2
